TPU v7x, 32 devices: a whole 2x2x4 slice. The times are simulated.
32 devices in a mesh: expert: 4 (over y, x), dp: 8 (over z, core).
Axes of the slice: x: 2, y: 2, z: 4, core: 2. Of those that a mesh axis runs over, the one named last changes fastest.
Arguments:
- routes: int32 [4096, 2], P(('expert', 'dp')), may hold values from 0 to 1, as said below
- expert_inputs: bfloat16 [8, 4, 512, 2048], P('dp', 'expert'), may hold values from -6 to 6
- hidden_grad: bfloat16 [8, 4, 512, 2048], P('dp', 'expert'), may hold values from -6 to 6
- weight: float32 [2048, 8192], P('dp', 'expert'), may hold values from -0.125 to 0.125
- moment_one: float32 [2048, 8192], P('dp', 'expert'), may hold values from -6 to 6
- moment_two: float32 [2048, 8192], P('dp', 'expert'), may hold values from 0.5 to 4
Outputs:
- token_grad: bfloat16 [4096, 2048], P(('expert', 'dp'))
- new_weight: float32 [2048, 8192], P('dp', 'expert')
- new_first: float32 [2048, 8192], P('dp', 'expert')
- new_second: float32 [2048, 8192], P('dp', 'expert')
Inputs may be any that keep to these rules, and one draw needn't show every extreme that they name: `routes`: each token names 2 different experts; the tokens of one device name one expert at most 128 times, and in every device's tokens some expert is named exactly 128 times.
All inputs are finite; a program needn't handle non-finite values.
Results may differ from a plain program's by a relative error of at most 0.0045.
The roundings to bfloat16 on the way count: a program that leaves them out, or rounds other values in their place, can miss the bound.
Values may be sent and summed in bfloat16 or wider, within the bound.
No kernel may reach another device: no remote copies, remote signals or barrier semaphores. Data moves between devices by JAX's collectives and lax.ppermute only.
A program may use at most 128 MiB of HBM per device.

v0:
```python
import jax
import jax.numpy as jnp
from jax import lax
from jax.sharding import PartitionSpec as P

beta_one = 0.9
beta_two = 0.95
learn_rate = 0.003
decay = 0.1
epsilon = 1e-08
loss_scale = 64.0
bias_one = 1.0 - (0.9**50) ** 2
bias_two = 1.0 - (0.95**50) ** 2


def adamw(weight, moment_one, moment_two, grad):
    new_first = beta_one * moment_one + (1.0 - beta_one) * grad
    new_second = beta_two * moment_two + (1.0 - beta_two) * grad * grad
    update = new_first / bias_one / (jnp.sqrt(new_second / bias_two) + epsilon)
    new_weight = weight - learn_rate * (update + decay * weight)
    return (new_weight, new_first, new_second)


def shards(routes, expert_inputs, hidden_grad, weight, moment_one, moment_two):
    n_expert = lax.axis_size("expert")
    experts = n_expert // 2
    slot_rows = expert_inputs.shape[2]
    capacity = slot_rows // n_expert
    width = expert_inputs.shape[3]
    tok_count = routes.shape[0]
    top_count = routes.shape[1]
    flat_routes = routes.reshape(-1)
    onehot = (flat_routes[:, None] == jnp.arange(experts, dtype=jnp.int32)[None, :]).astype(
        jnp.int32
    )
    running = jnp.cumsum(onehot, axis=0)
    slots = jnp.sum((running - 1) * onehot, axis=1).reshape(tok_count, top_count)
    counts = jnp.sum(onehot, axis=0)
    all_counts = lax.all_gather(counts[None, :], "expert", axis=0, tiled=True)
    my_expert = lax.axis_index("expert") // 2
    chosen = jnp.arange(experts, dtype=jnp.int32)[None, :] == my_expert
    my_counts = jnp.sum(jnp.where(chosen, all_counts, 0), axis=1)
    valid = (jnp.arange(capacity, dtype=jnp.int32)[None, :] < my_counts[:, None]).reshape(-1)
    inputs_flat = expert_inputs.reshape(slot_rows, width)
    grad_flat = hidden_grad.reshape(slot_rows, -1)
    masked = jnp.where(valid[:, None], grad_flat, jnp.zeros_like(grad_flat))
    wbf = weight.astype(jnp.bfloat16)
    partial_rows = lax.dot_general(
        masked,
        lax.all_gather(wbf, "dp", axis=0, tiled=True),
        (((1,), (1,)), ((), ())),
        preferred_element_type=jnp.float32,
    )
    sent = partial_rows.reshape(n_expert, capacity, width)
    received = lax.all_to_all(sent, "expert", split_axis=0, concat_axis=0, tiled=True)
    paired = jnp.sum(received.reshape(experts, 2, capacity, width), axis=1).astype(jnp.bfloat16)
    picked = paired[routes, slots]
    token_grad = jnp.sum(picked.astype(jnp.float32), axis=1).astype(jnp.bfloat16)
    owned = lax.psum_scatter(
        lax.dot_general(
            inputs_flat, masked, (((0,), (0,)), ((), ())), preferred_element_type=jnp.float32
        ).astype(jnp.bfloat16),
        "dp",
        scatter_dimension=0,
        tiled=True,
    ).astype(jnp.float32)
    new_weight, new_first, new_second = adamw(weight, moment_one, moment_two, owned / loss_scale)
    return (token_grad, new_weight, new_first, new_second)


def solution(mesh):
    in_specs = (
        P(("expert", "dp"), None),
        P("dp", "expert", None, None),
        P("dp", "expert", None, None),
        P("dp", "expert"),
        P("dp", "expert"),
        P("dp", "expert"),
    )
    out_specs = (P(("expert", "dp"), None), P("dp", "expert"), P("dp", "expert"), P("dp", "expert"))
    return jax.shard_map(shards, mesh=mesh, in_specs=in_specs, out_specs=out_specs, check_vma=False)
```

profile of v0, /device:TPU:0, one launch (start us, length us, event | category | flops | bytes accessed | tf_op | source)
XLA Modules:
  0.0 221.4 jit_solution(1023216353679421165)
XLA Ops:
  7.2 2.9 %convert_element_type.25 = bf16[256,2048]{1,0:T(8,128)(2,1)} convert(f32[256,2048]{1,0:T(8,128)} %param.9) | non-fusion elementwise | flops 524288 | bytes 3145728 | tf_op jit(solution)/shard_map/convert_element_type | solution.py:47
  10.2 0.1 copy.31
  10.3 0.1 eq.42
  10.4 0.1 eq.38
  10.6 0.6 reduce-window.6
  11.2 0.2 slice_reduce_fusion
  11.4 0.2 reduce-window.9
  11.6 0.6 dynamic-slice
  12.9 0.1 fusion.14
  13.1 0.2 dynamic-update-slice
  13.3 8.8 %all-reduce = s32[8]{0:T(128)S(1)} all-reduce(s32[8]{0:T(128)S(1)} %dynamic-update-slice), channel_id=2, replica_groups=mesh['expert'=4,'dp'=8] {'expert'}, use_global_device_ids=true, to_apply=%add | all-reduce | flops 8 | bytes 64
  22.1 0.1 reshape.114
  22.2 0.1 select_reduce_fusion
  22.4 8.8 %convert_bitcast_fusion = bf16[2048,2048]{0,1:T(8,128)(2,1)} fusion(bf16[1,1,512,2048]{3,2,1,0:T(8,128)(2,1)S(1)} %copy-done, bf16[1,1,512,2048]{3,2,1,0:T(8,128)(2,1)} %param.8, pred[512]{0:T(512)(128)(4,1)S(1)} %get-tuple-element.21), kind=kOutput, calls=%fused_computation.3 | convolution fusion | flops 4300210176 | bytes 12583424 | tf_op jit(solution)/shard_map/dot_general | solution.py:60
  31.2 63.8 %all-gather.3.cloned.1.call-done = bf16[2048,2048]{1,0:T(8,128)(2,1)} async-done(((bf16[256,2048]{1,0:T(8,128)(2,1)}), bf16[2048,2048]{1,0:T(8,128)(2,1)}) %all-gather.3.cloned.1.call-update) | async-done | bytes 8388624 | tf_op jit(solution)/shard_map/all_gather | solution.py:50
  95.0 10.5 %fusion = f32[4,128,2048]{2,1,0:T(8,128)} fusion(bf16[2048,2048]{1,0:T(8,128)(2,1)} %all-gather.3.cloned.1.call-done, bf16[4,128,2048]{2,1,0:T(8,128)(2,1)} %bitcast.39, pred[4,128]{1,0:T(4,128)(4,1)S(1)} %get-tuple-element.22), kind=kOutput, calls=%fused_computation.1 | convolution fusion | flops 4296015872 | bytes 14680576 | tf_op jit(solution)/shard_map/dot_general | solution.py:48
  105.6 5.1 %all-to-all-start = ((f32[4,128,2048]{2,1,0:T(8,128)}), f32[4,128,2048]{2,1,0:T(8,128)}, u32[]{:S(2)}, u32[]{:S(2)}) async-start(f32[4,128,2048]{2,1,0:T(8,128)} %fusion), calls=%async_computation | async-start | bytes 8388608 | tf_op jit(solution)/shard_map/all_to_all | solution.py:55
  110.7 2.9 %copy.40 = f32[256,2048]{0,1:T(8,128)} copy(f32[256,2048]{1,0:T(8,128)} %param.9) | data formatting | bytes 4194304 | tf_op args[3]
  113.6 0.1 reshape.106
  113.8 0.1 copy.36
  113.9 0.1 reshape.108
  114.1 2.9 %copy.37 = f32[256,2048]{0,1:T(8,128)} copy(f32[256,2048]{1,0:T(8,128)} %param.10) | data formatting | bytes 4194304 | tf_op args[4]
  117.0 2.9 %copy.38 = f32[256,2048]{0,1:T(8,128)} copy(f32[256,2048]{1,0:T(8,128)} %param.11) | data formatting | bytes 4194304 | tf_op args[5]
  119.9 65.6 %reduce-scatter.2.cloned.1.call-done = bf16[256,2048]{0,1:T(8,128)(2,1)} async-done(((bf16[2048,2048]{0,1:T(8,128)(2,1)}), bf16[256,2048]{0,1:T(8,128)(2,1)}) %reduce-scatter.2.cloned.1.call-update) | async-done | bytes 1048592 | tf_op jit(solution)/shard_map/reduce_scatter | solution.py:59
  185.5 7.0 %multiply_subtract_fusion = (f32[256,2048]{0,1:T(8,128)}, f32[256,2048]{0,1:T(8,128)}, f32[256,2048]{0,1:T(8,128)}) fusion(f32[256,2048]{0,1:T(8,128)} %copy.40, bf16[256,2048]{0,1:T(8,128)(2,1)} %reduce-scatter.2.cloned.1.call-done, f32[256,2048]{0,1:T(8,128)} %copy.37, f32[256,2048]{0,1:T(8,128)} %copy.38), kind=kLoop, calls=%fused_computation.13 | loop fusion | flops 8912896 | bytes 13631488 | tf_op jit(solution)/shard_map/sub | solution.py:20
  192.5 2.9 %copy.41 = f32[256,2048]{1,0:T(8,128)} copy(f32[256,2048]{0,1:T(8,128)} %get-tuple-element.18) | data formatting | bytes 4194304
  195.4 2.9 %copy.42 = f32[256,2048]{1,0:T(8,128)} copy(f32[256,2048]{0,1:T(8,128)} %get-tuple-element.19) | data formatting | bytes 4194304
  198.2 2.9 %copy.43 = f32[256,2048]{1,0:T(8,128)} copy(f32[256,2048]{0,1:T(8,128)} %get-tuple-element.20) | data formatting | bytes 4194304
  201.1 2.7 %bitcast_reduce_fusion = bf16[2,128,2048]{2,1,0:T(8,128)(2,1)S(1)} fusion(f32[4,128,2048]{2,1,0:T(8,128)} %all-to-all-done), kind=kLoop, calls=%fused_computation.4 | loop fusion | flops 524288 | bytes 5242880 | tf_op jit(solution)/shard_map/reduce_sum | solution.py:56
  203.9 5.3 %gather_fusion = bf16[256,2048]{1,0:T(8,128)(2,1)} fusion(bf16[2,128,2048]{2,1,0:T(8,128)(2,1)S(1)} %bitcast_reduce_fusion, s32[256]{0:T(256)S(1)} %reshape.108), kind=kCustom, calls=%fused_computation | custom fusion | bytes 2099200 | tf_op jit(solution)/shard_map/gather | solution.py:57
  209.2 1.7 reshape.111
  210.9 3.6 %reduce_sum.52 = bf16[128,2048]{1,0:T(8,128)(2,1)} reduce(bf16[128,2,2048]{2,1,0:T(2,128)(2,1)S(1)} %reshape.111, bf16[]{:T(256)} %constant.46.clone.1), dimensions={1}, to_apply=%region_6.7 | reduce | flops 262144 | bytes 1572866 | tf_op jit(solution)/shard_map/reduce_sum | solution.py:58
  (18 shorter events, 0.4 us)
Async XLA Ops:
  7.2 15.2 %copy-start = (bf16[1,1,512,2048]{3,2,1,0:T(8,128)(2,1)S(1)}, bf16[1,1,512,2048]{3,2,1,0:T(8,128)(2,1)}, u32[]{:S(2)}) copy-start(bf16[1,1,512,2048]{3,2,1,0:T(8,128)(2,1)} %param.7) | copy-start | bytes 6291460
  7.2 4.4 %copy-start.2 = (u32[32]{0:T(128)S(1)}, u32[32]{0:T(128)}, u32[]{:S(2)}) copy-start(u32[32]{0:T(128)} %constant.77) | copy-start | bytes 388
  7.2 3.0 %copy-start.1 = (s32[128,2]{0,1:T(2,128)S(1)}, s32[128,2]{0,1:T(2,128)}, u32[]{:S(2)}) copy-start(s32[128,2]{0,1:T(2,128)} %param.6) | copy-start | bytes 3076
  7.2 87.8 %all-gather.3.cloned.1.call-start = ((), (), s32[]{:S(2)}) async-start(), calls=%async_computation.2 | async-start | bytes 9437184 | tf_op jit(solution)/shard_map/all_gather | solution.py:50
  10.1 175.4 %reduce-scatter.2.cloned.1.call-start = ((), (), s32[]{:S(2)}) async-start(), calls=%async_computation.3 | async-start | bytes 9437184 | tf_op jit(solution)/shard_map/reduce_scatter | solution.py:59
  105.6 95.5 %all-to-all-start = ((f32[4,128,2048]{2,1,0:T(8,128)}), f32[4,128,2048]{2,1,0:T(8,128)}, u32[]{:S(2)}, u32[]{:S(2)}) async-start(f32[4,128,2048]{2,1,0:T(8,128)} %fusion), calls=%async_computation | async-start | bytes 8388608 | tf_op jit(solution)/shard_map/all_to_all | solution.py:55
Sparse Core Ops, SparseCore 0:
  10.2 84.7 all-gather.2
  97.3 88.1 reduce-scatter.1
where the time goes:
time: 222 us; the launch traced here: 221 us
  waiting for transfers between devices  129 us (58%)
  local copies, waits for them, and re-layouts  26.4 us (12%)
  matrix products  19.4 us (9%)
  other arithmetic  17.4 us (8%)
  between operations  14.8 us (7%)
  blocking collectives  8.82 us (4%)
  starting transfers between devices  5.2 us (2%)
    reduce_scatter x1, waiting for transfers between devices, shards(): lax.psum_scatter(lax.dot_general(inputs_flat, masked, (((0,), (0,)), ((),...  65.6 us
    all_gather x1, waiting for transfers between devices, shards(): lax.all_gather(wbf, 'dp', axis=0, tiled=True)  63.8 us
    unnamed x16, local copies, waits for them, and re-layouts  18.3 us
    dot_general x1, matrix products, shards(): lax.dot_general(masked, lax.all_gather(wbf, 'dp', axis=0, tiled=True), ((...  10.5 us
    unnamed x1, blocking collectives  8.82 us
    dot_general x1, matrix products, shards(): lax.dot_general(inputs_flat, masked, (((0,), (0,)), ((), ())), preferred_...  8.81 us
    gather x2, local copies, waits for them, and re-layouts, shards(): picked = paired[routes, slots]  7.06 us
    sub x1, other arithmetic, adamw(): new_weight = weight - learn_rate * (update + decay * weight)  6.97 us
  transfers between devices with their start and end apart: 3, of which 2 were waited for; matrix products, arithmetic and copies ran while one was open for 21% of the time, Pallas kernels for 0%

commit v1 on v0

--- a/solution.py
+++ b/solution.py
@@ -11,6 +11,18 @@
 loss_scale = 64.0
 bias_one = 1.0 - (0.9**50) ** 2
 bias_two = 1.0 - (0.95**50) ** 2
+
+
+def gather_by_bits(x, axis, dim):
+    ways, here, step = (lax.axis_size(axis), lax.axis_index(axis), x.shape[dim])
+    line, have = (x, 1)
+    while have < ways:
+        line = jnp.concatenate(
+            [line, lax.ppermute(line, axis, [(d, (d - have) % ways) for d in range(ways)])],
+            axis=dim,
+        )
+        have = 2 * have
+    return jnp.roll(line, here * step, axis=dim)
 
 
 def adamw(weight, moment_one, moment_two, grad):
@@ -47,7 +59,7 @@
     wbf = weight.astype(jnp.bfloat16)
     partial_rows = lax.dot_general(
         masked,
-        lax.all_gather(wbf, "dp", axis=0, tiled=True),
+        gather_by_bits(wbf, "dp", 0),
         (((1,), (1,)), ((), ())),
         preferred_element_type=jnp.float32,
     )

time: 222 us -> 462 us (2.08)
  waiting for transfers between devices: 129 us -> 353 us
  local copies, waits for them, and re-layouts: 26.4 us -> 41.2 us
    ppermute x0 -> x3, waiting for transfers between devices: none -> 312 us  [gather_by_bits(): lax.ppermute(line, axis, [(d, (d - have) % ways) for d in range(ways)])]
    reduce_scatter x1, waiting for transfers between devices: 65.6 us -> 0.01 us  [shards(): lax.psum_scatter(lax.dot_general(inputs_flat, masked, (((0,), (0,)), ((),...]
    all_gather x1 -> x0, waiting for transfers between devices: 63.8 us -> none  [shards(): lax.all_gather(wbf, 'dp', axis=0, tiled=True)]
    all_to_all x1, waiting for transfers between devices: 0.01 us -> 40.6 us  [shards(): lax.all_to_all(sent, 'expert', split_axis=0, concat_axis=0, tiled=True)]
    unnamed x16 -> x38, local copies, waits for them, and re-layouts: 18.3 us -> 29.4 us
    concatenate x0 -> x1, local copies, waits for them, and re-layouts: none -> 4.88 us  [gather_by_bits(): return jnp.roll(line, here * step, axis=dim)]
  transfers between devices with their start and end apart: 3 -> 5, of which waited for: 2 -> 4; matrix products, arithmetic and copies ran while one was open for 21% -> 11% of each run, Pallas kernels for 0% -> 0%
where the time goes in v1:
time: 462 us; the launch traced here: 461 us
  waiting for transfers between devices  353 us (76%)
  local copies, waits for them, and re-layouts  41.2 us (9%)
  other arithmetic  18.5 us (4%)
  matrix products  18.2 us (4%)
  between operations  14.8 us (3%)
  blocking collectives  8.82 us (2%)
  starting transfers between devices  6.87 us (1%)
    ppermute x3, waiting for transfers between devices, gather_by_bits(): lax.ppermute(line, axis, [(d, (d - have) % ways) for d in range(ways)])  312 us
    all_to_all x1, waiting for transfers between devices, shards(): lax.all_to_all(sent, 'expert', split_axis=0, concat_axis=0, tiled=True)  40.6 us
    unnamed x38, local copies, waits for them, and re-layouts  29.4 us
    dot_general x1, matrix products, shards(): lax.dot_general(masked, gather_by_bits(wbf, 'dp', 0), (((1,), (1,)), ((),...  9.56 us
  transfers between devices with their start and end apart: 5, of which 4 were waited for; matrix products, arithmetic and copies ran while one was open for 11% of the time, Pallas kernels for 0%

profile of v1, /device:TPU:0, one launch (start us, length us, event | category | flops | bytes accessed | tf_op | source)
XLA Modules:
  0.0 461.2 jit_solution(18134090466026768931)
XLA Ops:
  7.2 0.9 copy.31
  9.7 1.2 dynamic-slice
  11.8 8.8 %all-reduce = s32[8]{0:T(128)S(1)} all-reduce(s32[8]{0:T(128)S(1)} %dynamic-update-slice), channel_id=2, replica_groups=mesh['expert'=4,'dp'=8] {'expert'}, use_global_device_ids=true, to_apply=%add | all-reduce | flops 8 | bytes 64
  20.9 8.7 %convert_bitcast_fusion = bf16[2048,2048]{0,1:T(8,128)(2,1)} fusion(bf16[1,1,512,2048]{3,2,1,0:T(8,128)(2,1)S(1)} %copy-done, bf16[1,1,512,2048]{3,2,1,0:T(8,128)(2,1)} %param.8, pred[512]{0:T(512)(128)(4,1)S(1)} %get-tuple-element.23), kind=kOutput, calls=%fused_computation.3 | convolution fusion | flops 4300210176 | bytes 12583424 | tf_op jit(solution)/shard_map/dot_general | solution.py:72
  29.6 1.6 copy-done.4
  31.2 1.2 constant_dynamic-update-slice_fusion.7
  32.3 1.0 collective-permute-start
  33.4 31.8 %collective-permute-done = bf16[256,2048]{1,0:T(8,128)(2,1)S(1)} collective-permute-done((bf16[256,2048]{1,0:T(8,128)(2,1)S(1)}, bf16[256,2048]{1,0:T(8,128)(2,1)S(1)}, u32[]{:S(2)}, u32[]{:S(2)}) %collective-permute-start) | collective-permute-done | bytes 1048608 | tf_op jit(solution)/shard_map/ppermute | solution.py:21
  66.0 92.1 %collective-permute-done.1 = bf16[512,2048]{1,0:T(8,128)(2,1)S(1)} collective-permute-done((bf16[512,2048]{1,0:T(8,128)(2,1)S(1)}, bf16[512,2048]{1,0:T(8,128)(2,1)S(1)}, u32[]{:S(2)}, u32[]{:S(2)}) %collective-permute-start.1) | collective-permute-done | bytes 2097184 | tf_op jit(solution)/shard_map/ppermute | solution.py:21
  158.1 2.3 pad_maximum_fusion
  160.4 1.1 constant_dynamic-update-slice_fusion.6
  161.5 1.4 constant_dynamic-update-slice_fusion.5
  163.0 188.2 %collective-permute-done.2 = bf16[1024,2048]{1,0:T(8,128)(2,1)} collective-permute-done((bf16[1024,2048]{1,0:T(8,128)(2,1)}, bf16[1024,2048]{1,0:T(8,128)(2,1)}, u32[]{:S(2)}, u32[]{:S(2)}) %collective-permute-start.2) | collective-permute-done | bytes 4194336 | tf_op jit(solution)/shard_map/ppermute | solution.py:21
  351.2 4.7 %constant_dynamic-update-slice_fusion.4 = bf16[4096,2048]{1,0:T(8,128)(2,1)} fusion(bf16[4096,2048]{1,0:T(8,128)(2,1)} %constant_dynamic-update-slice_fusion.5, bf16[1024,2048]{1,0:T(8,128)(2,1)} %collective-permute-done.2), kind=kLoop, calls=%fused_computation.27 | loop fusion | bytes 8388608
  355.9 1.1 constant_dynamic-update-slice_fusion.3
  357.1 1.0 constant_dynamic-update-slice_fusion.2
  358.1 1.4 constant_dynamic-update-slice_fusion.1
  359.5 4.9 %constant_dynamic-update-slice_fusion = bf16[4096,2048]{1,0:T(8,128)(2,1)} fusion(bf16[4096,2048]{1,0:T(8,128)(2,1)} %constant_dynamic-update-slice_fusion.1, bf16[1024,2048]{1,0:T(8,128)(2,1)} %collective-permute-done.2), kind=kLoop, calls=%fused_computation.23 | loop fusion | bytes 8388608 | tf_op jit(solution)/shard_map/jit(_roll_dynamic)/concatenate | solution.py:25
  364.4 9.6 %fusion = f32[4,128,2048]{2,1,0:T(8,128)} fusion(bf16[4096,2048]{1,0:T(8,128)(2,1)} %constant_dynamic-update-slice_fusion, s32[]{:T(128)S(6)} %select_n.48, bf16[4,128,2048]{2,1,0:T(8,128)(2,1)S(1)} %bitcast.39, pred[4,128]{1,0:T(4,128)(4,1)S(1)} %get-tuple-element.24), kind=kOutput, calls=%fused_computation.1 | convolution fusion | flops 4296015872 | bytes 14680580 | tf_op jit(solution)/shard_map/dot_general | solution.py:60
  374.0 5.2 %all-to-all-start = ((f32[4,128,2048]{2,1,0:T(8,128)}), f32[4,128,2048]{2,1,0:T(8,128)}, u32[]{:S(2)}, u32[]{:S(2)}) async-start(f32[4,128,2048]{2,1,0:T(8,128)} %fusion), calls=%async_computation | async-start | bytes 8388608 | tf_op jit(solution)/shard_map/all_to_all | solution.py:67
  379.2 1.8 copy.40
  381.5 3.0 copy.37
  384.5 1.8 copy.38
  386.3 40.6 %all-to-all-done = f32[4,128,2048]{2,1,0:T(8,128)} async-done(((f32[4,128,2048]{2,1,0:T(8,128)}), f32[4,128,2048]{2,1,0:T(8,128)}, u32[]{:S(2)}, u32[]{:S(2)}) %all-to-all-start) | async-done | bytes 4194336 | tf_op jit(solution)/shard_map/all_to_all | solution.py:67
  426.9 2.7 bitcast_reduce_fusion
  429.7 4.3 gather_fusion
  434.0 1.6 reshape.111
  435.6 4.6 reduce_sum.52
  440.2 6.3 %multiply_subtract_fusion = (f32[256,2048]{0,1:T(8,128)}, f32[256,2048]{0,1:T(8,128)}, f32[256,2048]{0,1:T(8,128)}) fusion(f32[256,2048]{0,1:T(8,128)S(1)} %copy-done.6, bf16[256,2048]{0,1:T(8,128)(2,1)} %reduce-scatter.2.cloned.1.call-done, f32[256,2048]{0,1:T(8,128)} %copy.37, f32[256,2048]{0,1:T(8,128)} %copy.38), kind=kLoop, calls=%fused_computation.16 | loop fusion | flops 8912896 | bytes 13631488 | tf_op jit(solution)/shard_map/sub | solution.py:32
  446.5 3.0 copy.41
  449.5 1.8 copy.42
  451.3 3.0 copy.43
  (46 shorter events, 3.4 us)
Async XLA Ops:
  7.2 13.8 %copy-start = (bf16[1,1,512,2048]{3,2,1,0:T(8,128)(2,1)S(1)}, bf16[1,1,512,2048]{3,2,1,0:T(8,128)(2,1)}, u32[]{:S(2)}) copy-start(bf16[1,1,512,2048]{3,2,1,0:T(8,128)(2,1)} %param.7) | copy-start | bytes 6291460
  7.2 433.0 %reduce-scatter.2.cloned.1.call-start = ((), (), s32[]{:S(2)}) async-start(), calls=%async_computation.2 | async-start | bytes 9437184 | tf_op jit(solution)/shard_map/reduce_scatter | solution.py:71
  29.6 1.6 copy-start.4
  32.3 125.8 %copy-start.2 = (bf16[256,2048]{1,0:T(8,128)(2,1)}, bf16[256,2048]{1,0:T(8,128)(2,1)S(1)}, u32[]{:S(2)}) copy-start(bf16[256,2048]{1,0:T(8,128)(2,1)S(1)} %get-tuple-element.22) | copy-start | bytes 3145732
  32.3 32.9 %collective-permute-start = (bf16[256,2048]{1,0:T(8,128)(2,1)S(1)}, bf16[256,2048]{1,0:T(8,128)(2,1)S(1)}, u32[]{:S(2)}, u32[]{:S(2)}) collective-permute-start(bf16[256,2048]{1,0:T(8,128)(2,1)S(1)} %get-tuple-element.22), channel_id=1, source_target_pairs={{0,7},{1,0},{2,1},{3,2},{4,3},{5,4},{6,5},{7,6},{8,15},{9,8},{10,9... | collective-permute-start | bytes 3145736 | tf_op jit(solution)/shard_map/ppermute | solution.py:21
  65.4 92.7 %collective-permute-start.1 = (bf16[512,2048]{1,0:T(8,128)(2,1)S(1)}, bf16[512,2048]{1,0:T(8,128)(2,1)S(1)}, u32[]{:S(2)}, u32[]{:S(2)}) collective-permute-start(bf16[512,2048]{1,0:T(8,128)(2,1)S(1)} %pad_maximum_fusion.1), channel_id=1, source_target_pairs={{0,6},{1,7},{2,0},{3,1},{4,2},{5,3},{6,4},{7,5},{8,14},{9,15},{10,... | collective-permute-start | bytes 6291464 | tf_op jit(solution)/shard_map/ppermute | solution.py:21
  160.4 190.8 %collective-permute-start.2 = (bf16[1024,2048]{1,0:T(8,128)(2,1)}, bf16[1024,2048]{1,0:T(8,128)(2,1)}, u32[]{:S(2)}, u32[]{:S(2)}) collective-permute-start(bf16[1024,2048]{1,0:T(8,128)(2,1)} %pad_maximum_fusion), channel_id=1, source_target_pairs={{0,4},{1,5},{2,6},{3,7},{4,0},{5,1},{6,2},{7,3},{8,12},{9,13},{10,... | collective-permute-start | bytes 12582920 | tf_op jit(solution)/shard_map/ppermute | solution.py:21
  163.0 193.0 %copy-start.3 = (bf16[256,2048]{1,0:T(8,128)(2,1)S(1)}, bf16[256,2048]{1,0:T(8,128)(2,1)}, u32[]{:S(2)}) copy-start(bf16[256,2048]{1,0:T(8,128)(2,1)} %copy-done.2) | copy-start | bytes 3145732
  359.5 4.9 %copy-start.10 = (bf16[1,1,512,2048]{3,2,1,0:T(8,128)(2,1)S(1)}, bf16[1,1,512,2048]{3,2,1,0:T(8,128)(2,1)}, u32[]{:S(2)}) copy-start(bf16[1,1,512,2048]{3,2,1,0:T(8,128)(2,1)} %param.8) | copy-start | bytes 6291460
  374.0 5.2 %copy-start.5 = (f32[256,2048]{1,0:T(8,128)S(1)}, f32[256,2048]{1,0:T(8,128)}, u32[]{:S(2)}) copy-start(f32[256,2048]{1,0:T(8,128)} %param.9) | copy-start | bytes 6291460
  374.0 53.0 %all-to-all-start = ((f32[4,128,2048]{2,1,0:T(8,128)}), f32[4,128,2048]{2,1,0:T(8,128)}, u32[]{:S(2)}, u32[]{:S(2)}) async-start(f32[4,128,2048]{2,1,0:T(8,128)} %fusion), calls=%async_computation | async-start | bytes 8388608 | tf_op jit(solution)/shard_map/all_to_all | solution.py:67
  379.2 2.0 copy-start.9
  381.5 3.0 copy-start.8
  434.0 6.2 %copy-start.6 = (f32[256,2048]{0,1:T(8,128)S(1)}, f32[256,2048]{0,1:T(8,128)}, u32[]{:S(2)}) copy-start(f32[256,2048]{0,1:T(8,128)} %copy.40) | copy-start | bytes 6291460
  446.5 3.0 copy-start.7
  451.3 3.0 copy-start.1
Sparse Core Ops, SparseCore 0:
  29.7 150.8 reduce-scatter.1
